TPU v7x, 128 devices: a whole 4x4x4 slice. The times are simulated.
128 devices in a mesh: group: 8 (over y, core), member: 16 (over x, z).
Axes of the slice: x: 4, y: 4, z: 4, core: 2. Of those that a mesh axis runs over, the one named last changes fastest.
Arguments:
- queries: bfloat16 [2048, 64, 576], P(('group', 'member')), may hold values from -240 to 240
- latent_cache: bfloat16 [2048, 128, 576], P(('group', 'member')), may hold values from -4 to 4
- new_key: bfloat16 [2048, 576], P(('group', 'member')), may hold values from -4 to 4
- parent_beam: int32 [2048], P(('group', 'member')), may hold values from 0 to 3
- value_up: bfloat16 [64, 512, 128], P('member'), may hold values from -0.25 to 0.25
- out_proj: bfloat16 [8192, 3584], P('member', 'group'), may hold values from -0.0625 to 0.0625
- residual: bfloat16 [2048, 3584], P('member', 'group'), may hold values from -6 to 6
- expert_ids: int32 [2048, 8], P('member'), may hold values from 0 to 127, all different within a row; in each aligned block of 128 rows (0 to 127, 128 to 255, ...) at most 16 rows name the same one
- route_gates: float32 [2048, 8], P('member'), may hold values from 0.1 to 0.6
- w_gate: bfloat16 [128, 3584, 1024], P(('group', 'member')), may hold values from -0.09375 to 0.09375
- w_up: bfloat16 [128, 3584, 1024], P(('group', 'member')), may hold values from -0.09375 to 0.09375
- w_down: bfloat16 [128, 1024, 3584], P(('group', 'member')), may hold values from -0.1875 to 0.1875
Outputs:
- layer_out: bfloat16 [2048, 3584], P('member', 'group')
Inputs may be any that keep to these rules, and one draw needn't show every extreme that they name: `expert_ids`: each row names 8 different experts. Within each aligned block of 128 rows no expert is named by more than 16 rows, a bound that some block reaches.
All inputs are finite; a program needn't handle non-finite values.
Results may differ from a plain program's by a relative error of at most 0.019.
Values may be sent and summed in bfloat16 or wider, within the bound.
No kernel may reach another device: no remote copies, remote signals or barrier semaphores. Data moves between devices by JAX's collectives and lax.ppermute only.
A program may use at most 128 MiB of HBM per device.

v0:
```python
import jax
import jax.numpy as jnp
from jax import lax
from jax.sharding import PartitionSpec as P

ROPE = 64
VHEAD = 128
TOP = 8
BEAM = 4


def per_device(
    queries,
    latent_cache,
    new_key,
    parent_beam,
    value_up,
    out_proj,
    residual,
    expert_ids,
    route_gates,
    w_gate,
    w_up,
    w_down,
):
    rows = queries.shape[0]
    latent = value_up.shape[1]
    members = lax.axis_size("member")
    groups = lax.axis_size("group")
    experts = groups * members
    columns = out_proj.shape[1]
    scale = (VHEAD + ROPE) ** (-0.5)
    local_rows = jnp.arange(rows, dtype=jnp.int32)
    parent = local_rows // BEAM * BEAM + parent_beam
    keys = jnp.concatenate([jnp.take(latent_cache, parent, axis=0), new_key[:, None, :]], axis=1)
    chunks = 2
    step = rows // chunks
    pieces = []
    for c in range(chunks):
        asked = queries[c * step : (c + 1) * step]
        held = keys[c * step : (c + 1) * step]
        scores = jnp.einsum("rhw,rcw->rhc", asked, held, preferred_element_type=jnp.float32) * scale
        shifted = jnp.exp(scores - jnp.max(scores, axis=-1, keepdims=True))
        weights = (shifted / jnp.sum(shifted, axis=-1, keepdims=True)).astype(jnp.bfloat16)
        latent_out = jnp.einsum(
            "rhc,rcl->rhl", weights, held[:, :, :latent], preferred_element_type=jnp.float32
        ).astype(jnp.bfloat16)
        by_heads = lax.all_to_all(latent_out, "member", split_axis=1, concat_axis=0, tiled=True)
        per_head = jnp.einsum(
            "rhl,hlv->rhv", by_heads, value_up, preferred_element_type=jnp.float32
        ).astype(jnp.bfloat16)
        per_head = per_head.reshape(per_head.shape[0], per_head.shape[1] * per_head.shape[2])
        partial_sums = jnp.dot(
            lax.all_gather(per_head, "group", axis=0, tiled=True),
            out_proj,
            preferred_element_type=jnp.float32,
        )
        arrived_sums = lax.all_to_all(
            partial_sums.astype(jnp.bfloat16).reshape(members, -1, columns),
            "member",
            split_axis=0,
            concat_axis=0,
            tiled=True,
        )
        summed = jnp.sum(arrived_sums.astype(jnp.float32), axis=0)
        pieces.append(summed.reshape(-1, step, columns))
    attention = jnp.stack(pieces, axis=1).reshape(-1, columns)
    hidden_in = (residual.astype(jnp.float32) + attention).astype(jnp.bfloat16)
    block_rows = hidden_in.shape[0]
    capacity = max(2, 2 * rows * TOP // members)
    flat_ids = expert_ids.reshape(-1)
    onehot = (flat_ids[:, None] == jnp.arange(experts, dtype=jnp.int32)[None, :]).astype(jnp.int32)
    ranking = jnp.sum((jnp.cumsum(onehot, axis=0) - onehot) * onehot, axis=1)
    slot_index = flat_ids * capacity + ranking
    positions = jnp.arange(experts * capacity, dtype=jnp.int32)
    matches = (positions[:, None] == slot_index[None, :]).reshape(
        experts * capacity, block_rows, TOP
    )
    send_map = jnp.any(matches, axis=2).astype(jnp.bfloat16)
    outgoing = jnp.dot(send_map, hidden_in, preferred_element_type=jnp.float32).astype(jnp.bfloat16)
    arrived = lax.all_to_all(
        outgoing.reshape(experts, capacity, columns),
        ("group", "member"),
        split_axis=0,
        concat_axis=0,
        tiled=True,
    )
    expert_rows = (
        arrived.reshape(groups, members, capacity, columns)
        .transpose(1, 2, 0, 3)
        .reshape(members * capacity, groups * columns)
    )
    gate = jnp.dot(expert_rows, w_gate[0], preferred_element_type=jnp.float32)
    upper = jnp.dot(expert_rows, w_up[0], preferred_element_type=jnp.float32)
    inner = (jax.nn.silu(gate) * upper).astype(jnp.bfloat16)
    results = jnp.dot(inner, w_down[0], preferred_element_type=jnp.float32).astype(jnp.bfloat16)
    arranged = (
        results.reshape(members, capacity, groups, columns)
        .transpose(2, 0, 1, 3)
        .reshape(experts, capacity, columns)
    )
    returned = lax.all_to_all(
        arranged, ("group", "member"), split_axis=0, concat_axis=0, tiled=True
    )
    returned = returned.reshape(experts * capacity, columns)
    picked = returned[slot_index.reshape(block_rows, TOP)].astype(jnp.float32)
    mixed = jnp.sum(route_gates[:, :, None] * picked, axis=1)
    return (hidden_in.astype(jnp.float32) + mixed).astype(jnp.bfloat16)


def solution(mesh):
    in_specs = (
        P(("group", "member"), None, None),
        P(("group", "member"), None, None),
        P(("group", "member"), None),
        P(("group", "member")),
        P("member", None, None),
        P("member", "group"),
        P("member", "group"),
        P("member", None),
        P("member", None),
        P(("group", "member"), None, None),
        P(("group", "member"), None, None),
        P(("group", "member"), None, None),
    )
    out_specs = P("member", "group")
    return jax.shard_map(
        per_device, mesh=mesh, in_specs=in_specs, out_specs=out_specs, check_vma=False
    )
```

profile of v0, /device:TPU:1, one launch (start us, length us, event | category | flops | bytes accessed | tf_op | source)
XLA Modules:
  0.0 237.2 jit_solution(4019409785269201127)
XLA Ops:
  8.2 2.3 gather_fusion
  10.5 4.3 %copy.88 = bf16[16,128,576]{2,1,0:T(8,128)(2,1)} copy(bf16[16,128,576]{1,2,0:T(8,128)(2,1)} %gather_fusion) | data formatting | bytes 4718592 | tf_op jit(solution)/shard_map/jit(_take)/gather | solution.py:35
  14.9 2.2 broadcast_select_fusion
  18.8 2.3 convolution_convert_fusion.4
  21.5 18.6 %all_to_all.56 = bf16[8,64,512]{2,0,1:T(8,128)(2,1)S(1)} all-to-all(bf16[8,64,512]{2,0,1:T(8,128)(2,1)S(1)} %copy.90), channel_id=1, replica_groups=mesh['group'=8,'member'=16] {'member'}, dimensions={1} | all-to-all | bytes 1048576 | tf_op jit(solution)/shard_map/all_to_all | solution.py:48
  41.1 2.2 fusion.28
  43.5 2.3 convolution_convert_fusion.3
  46.1 12.5 %all_to_all.57 = bf16[8,64,512]{2,0,1:T(8,128)(2,1)S(1)} all-to-all(bf16[8,64,512]{2,0,1:T(8,128)(2,1)S(1)} %copy.94), channel_id=1, replica_groups=mesh['group'=8,'member'=16] {'member'}, dimensions={1} | all-to-all | bytes 1048576 | tf_op jit(solution)/shard_map/all_to_all | solution.py:48
  59.6 4.7 %all-gather.3.cloned.1.call-done = bf16[1024,512]{0,1:T(8,128)(2,1)} async-done(((bf16[128,512]{0,1:T(8,128)(2,1)}), bf16[1024,512]{0,1:T(8,128)(2,1)}) %all-gather.3.cloned.1.call-update) | async-done | bytes 1048592 | tf_op jit(solution)/shard_map/all_gather | solution.py:54
  67.5 6.7 %all-to-all-start.1 = ((bf16[16,64,448]{2,1,0:T(8,128)(2,1)}), bf16[16,64,448]{2,1,0:T(8,128)(2,1)S(1)}, u32[]{:S(2)}, u32[]{:S(2)}) async-start(bf16[16,64,448]{2,1,0:T(8,128)(2,1)} %bitcast.7), calls=%async_computation.1 | async-start | bytes 2097152 | tf_op jit(solution)/shard_map/all_to_all | solution.py:58
  74.8 15.5 %all-gather.5.cloned.1.call-done = bf16[1024,512]{0,1:T(8,128)(2,1)} async-done(((bf16[128,512]{0,1:T(8,128)(2,1)}), bf16[1024,512]{0,1:T(8,128)(2,1)}) %all-gather.5.cloned.1.call-update) | async-done | bytes 1048592 | tf_op jit(solution)/shard_map/all_gather | solution.py:54
  93.4 6.7 %all-to-all-start.3 = ((bf16[16,64,448]{2,1,0:T(8,128)(2,1)}), bf16[16,64,448]{2,1,0:T(8,128)(2,1)S(1)}, u32[]{:S(2)}, u32[]{:S(2)}) async-start(bf16[16,64,448]{2,1,0:T(8,128)(2,1)} %bitcast.15), calls=%async_computation.3 | async-start | bytes 2097152 | tf_op jit(solution)/shard_map/all_to_all | solution.py:58
  101.0 7.4 %fusion.2 = pred[2048,128]{1,0:T(8,128)(4,1)S(1)} fusion(s32[128,8]{0,1:T(8,128)S(1)} %get-tuple-element.6), kind=kLoop, calls=%fused_computation.5 | loop fusion | flops 3932160 | bytes 266240 | tf_op jit(solution)/shard_map/reduce_or | solution.py:79
  108.6 7.3 %all-to-all-done.3 = bf16[16,64,448]{2,1,0:T(8,128)(2,1)S(1)} async-done(((bf16[16,64,448]{2,1,0:T(8,128)(2,1)}), bf16[16,64,448]{2,1,0:T(8,128)(2,1)S(1)}, u32[]{:S(2)}, u32[]{:S(2)}) %all-to-all-start.3) | async-done | bytes 917536 | tf_op jit(solution)/shard_map/all_to_all | solution.py:58
  118.1 2.8 %copy.105 = bf16[2048,448]{1,0:T(8,128)(2,1)S(1)} copy(bf16[2048,448]{0,1:T(8,128)(2,1)} %convolution_convert_fusion) | data formatting | bytes 3670016 | tf_op jit(solution)/shard_map/convert_element_type | solution.py:80
  120.9 37.5 %all_to_all.58 = bf16[128,16,448]{2,1,0:T(8,128)(2,1)S(1)} all-to-all(bf16[128,16,448]{2,1,0:T(8,128)(2,1)S(1)} %bitcast.86), channel_id=1, replica_groups=mesh['group'=8,'member'=16] {'group','member'}, dimensions={0} | all-to-all | bytes 3670016 | tf_op jit(solution)/shard_map/all_to_all | solution.py:81
  159.9 3.3 %reshape.88 = bf16[256,3584]{1,0:T(8,128)(2,1)} reshape(bf16[16,16,8,448]{3,2,1,0:T(8,128)(2,1)S(1)} %bitcast.88) | data formatting | bytes 3670016 | tf_op jit(solution)/shard_map/reshape | solution.py:91
  163.2 6.8 %fusion.7 = f32[256,1024]{1,0:T(8,128)} fusion(bf16[256,3584]{1,0:T(8,128)(2,1)} %reshape.88, bf16[1,3584,1024]{2,1,0:T(8,128)(2,1)} %param.21), kind=kOutput, calls=%fused_computation.10 | convolution fusion | flops 1879048192 | bytes 10223616 | tf_op jit(solution)/shard_map/dot_general | solution.py:93
  170.0 10.8 %fusion.9 = bf16[256,3584]{1,0:T(8,128)(2,1)} fusion(bf16[1,1024,3584]{2,1,0:T(8,128)(2,1)} %param.23, bf16[256,3584]{1,0:T(8,128)(2,1)S(1)} %copy-done.4, bf16[1,3584,1024]{2,1,0:T(8,128)(2,1)} %param.22, f32[256,1024]{1,0:T(8,128)} %fusion.7), kind=kOutput, calls=%fused_computation.12 | convolution fusion | flops 3760586752 | bytes 19398656 | tf_op jit(solution)/shard_map/dot_general | solution.py:96
  180.8 3.9 %reshape.89 = bf16[16,16,8,448]{3,2,1,0:T(8,128)(2,1)S(1)} reshape(bf16[256,3584]{1,0:T(8,128)(2,1)} %fusion.9) | data formatting | bytes 3670016 | tf_op jit(solution)/shard_map/reshape | solution.py:98
  184.7 2.0 copy.107
  186.7 5.8 %all-to-all-start.5 = ((bf16[128,16,448]{2,1,0:T(8,128)(2,1)}), bf16[128,16,448]{2,1,0:T(8,128)(2,1)}, u32[]{:S(2)}, u32[]{:S(2)}) async-start(bf16[128,16,448]{2,1,0:T(8,128)(2,1)} %bitcast.28), calls=%async_computation.5 | async-start | bytes 4194304 | tf_op jit(solution)/shard_map/all_to_all | solution.py:102
  193.5 28.5 %all-to-all-done.5 = bf16[128,16,448]{2,1,0:T(8,128)(2,1)} async-done(((bf16[128,16,448]{2,1,0:T(8,128)(2,1)}), bf16[128,16,448]{2,1,0:T(8,128)(2,1)}, u32[]{:S(2)}, u32[]{:S(2)}) %all-to-all-start.5) | async-done | bytes 1835040 | tf_op jit(solution)/shard_map/all_to_all | solution.py:102
  222.0 6.0 %gather_fusion.1 = bf16[1024,448]{1,0:T(8,128)(2,1)S(1)} fusion(bf16[2048,448]{1,0:T(8,128)(2,1)} %bitcast.29, s32[1024]{0:T(1024)S(1)} %broadcast_clamp_fusion), kind=kCustom, calls=%fused_computation.1 | custom fusion | bytes 1839104 | tf_op jit(solution)/shard_map/gather | solution.py:106
  (70 shorter events, 21.2 us)
Async XLA Ops:
  6.5 1.7 copy-start
  6.5 57.8 %all-gather.3.cloned.1.call-start = ((), (), s32[]{:S(2)}) async-start(), calls=%async_computation.6 | async-start | bytes 1179648 | tf_op jit(solution)/shard_map/all_gather | solution.py:54
  10.5 4.3 %copy-start.6 = (bf16[16,576]{1,0:T(8,128)(2,1)S(1)}, bf16[16,576]{1,0:T(8,128)(2,1)}, u32[]{:S(2)}) copy-start(bf16[16,576]{1,0:T(8,128)(2,1)} %param.14) | copy-start | bytes 55300
  14.9 2.2 copy-start.9
  17.1 1.5 copy-start.2
  18.8 21.2 %copy-start.3 = (bf16[4,512,128]{2,1,0:T(8,128)(2,1)S(1)}, bf16[4,512,128]{2,1,0:T(8,128)(2,1)}, u32[]{:S(2)}) copy-start(bf16[4,512,128]{2,1,0:T(8,128)(2,1)} %param.16) | copy-start | bytes 1572868
  41.1 49.2 %all-gather.5.cloned.1.call-start = ((), (), s32[]{:S(2)}) async-start(), calls=%async_computation.7 | async-start | bytes 1179648 | tf_op jit(solution)/shard_map/all_gather | solution.py:54
  45.8 18.5 %copy-start.10 = (bf16[512,448]{0,1:T(8,128)(2,1)S(1)}, bf16[512,448]{0,1:T(8,128)(2,1)}, u32[]{:S(2)}) copy-start(bf16[512,448]{0,1:T(8,128)(2,1)} %param.17) | copy-start | bytes 1376260
  66.2 8.0 %copy-start.7 = (s32[128,8]{0,1:T(8,128)S(1)}, s32[128,8]{0,1:T(8,128)}, u32[]{:S(2)}) copy-start(s32[128,8]{0,1:T(8,128)} %param.19) | copy-start | bytes 12292
  67.5 25.9 %all-to-all-start.1 = ((bf16[16,64,448]{2,1,0:T(8,128)(2,1)}), bf16[16,64,448]{2,1,0:T(8,128)(2,1)S(1)}, u32[]{:S(2)}, u32[]{:S(2)}) async-start(bf16[16,64,448]{2,1,0:T(8,128)(2,1)} %bitcast.7), calls=%async_computation.1 | async-start | bytes 2097152 | tf_op jit(solution)/shard_map/all_to_all | solution.py:58
  92.1 8.2 %copy-start.5 = (bf16[128,448]{0,1:T(8,128)(2,1)S(1)}, bf16[128,448]{0,1:T(8,128)(2,1)}, u32[]{:S(2)}) copy-start(bf16[128,448]{0,1:T(8,128)(2,1)} %param.18) | copy-start | bytes 344068
  93.4 22.5 %all-to-all-start.3 = ((bf16[16,64,448]{2,1,0:T(8,128)(2,1)}), bf16[16,64,448]{2,1,0:T(8,128)(2,1)S(1)}, u32[]{:S(2)}, u32[]{:S(2)}) async-start(bf16[16,64,448]{2,1,0:T(8,128)(2,1)} %bitcast.15), calls=%async_computation.3 | async-start | bytes 2097152 | tf_op jit(solution)/shard_map/all_to_all | solution.py:58
  163.2 6.8 %copy-start.4 = (bf16[256,3584]{1,0:T(8,128)(2,1)S(1)}, bf16[256,3584]{1,0:T(8,128)(2,1)}, u32[]{:S(2)}) copy-start(bf16[256,3584]{1,0:T(8,128)(2,1)} %reshape.88) | copy-start | bytes 5505028
  186.7 6.1 %copy-start.8 = (f32[128,8]{0,1:T(8,128)S(1)}, f32[128,8]{0,1:T(8,128)}, u32[]{:S(2)}) copy-start(f32[128,8]{0,1:T(8,128)} %param.20) | copy-start | bytes 12292
  186.7 35.3 %all-to-all-start.5 = ((bf16[128,16,448]{2,1,0:T(8,128)(2,1)}), bf16[128,16,448]{2,1,0:T(8,128)(2,1)}, u32[]{:S(2)}, u32[]{:S(2)}) async-start(bf16[128,16,448]{2,1,0:T(8,128)(2,1)} %bitcast.28), calls=%async_computation.5 | async-start | bytes 4194304 | tf_op jit(solution)/shard_map/all_to_all | solution.py:102
  222.0 8.4 %copy-start.1 = (bf16[16,128,576]{1,2,0:T(8,128)(2,1)S(1)}, bf16[16,128,576]{1,2,0:T(8,128)(2,1)}, u32[]{:S(2)}) copy-start(bf16[16,128,576]{1,2,0:T(8,128)(2,1)} %param.13) | copy-start | bytes 7077892
Sparse Core Ops, SparseCore 0:
  41.2 23.0 all-gather.2
  66.0 24.2 all-gather.4
where the time goes:
time: 238 us; the launch traced here: 237 us
  blocking collectives  68.6 us (29%)
  waiting for transfers between devices  55.9 us (23%)
  local copies, waits for them, and re-layouts  33.5 us (14%)
  matrix products  32.7 us (14%)
  starting transfers between devices  19.2 us (8%)
  between operations  13.7 us (6%)
  other arithmetic  13.5 us (6%)
    all_to_all x1, blocking collectives, per_device(): lax.all_to_all(outgoing.reshape(experts, capacity, columns), ('group', 'm...  37.5 us
    all_to_all x2, blocking collectives, per_device(): lax.all_to_all(latent_out, 'member', split_axis=1, concat_axis=0, tiled=T...  31.1 us
    all_to_all x1, waiting for transfers between devices, per_device(): lax.all_to_all(arranged, ('group', 'member'), split_axis=0, concat_axis=0...  28.5 us
    all_gather x2, waiting for transfers between devices, per_device(): lax.all_gather(per_head, 'group', axis=0, tiled=True)  20.2 us
    all_to_all x2, starting transfers between devices, per_device(): lax.all_to_all(partial_sums.astype(jnp.bfloat16).reshape(members, -1, col...  13.4 us
    dot_general x1, matrix products, per_device(): jnp.dot(inner, w_down[0], preferred_element_type=jnp.float32)  10.8 us
    reduce_or x1, other arithmetic, per_device(): send_map = jnp.any(matches, axis=2).astype(jnp.bfloat16)  7.43 us
    all_to_all x2, waiting for transfers between devices, per_device(): lax.all_to_all(partial_sums.astype(jnp.bfloat16).reshape(members, -1, col...  7.28 us
  transfers between devices with their start and end apart: 5, of which 4 were waited for; matrix products, arithmetic and copies ran while one was open for 9% of the time, Pallas kernels for 0%

commit v1 on v0

--- a/solution.py
+++ b/solution.py
@@ -7,6 +7,24 @@
 VHEAD = 128
 TOP = 8
 BEAM = 4
+
+
+def gather_around(value, axis, dim):
+    ways, here, lap = (lax.axis_size(axis), lax.axis_index(axis), value.shape[dim])
+    shape = [n * ways if d == dim else n for d, n in enumerate(value.shape)]
+    full = lax.dynamic_update_slice_in_dim(
+        jnp.zeros(shape, value.dtype), value, here * lap, axis=dim
+    )
+    going_up = going_down = value
+    for far in range(1, ways // 2 + 1):
+        going_up = lax.ppermute(going_up, axis, [(d, (d + 1) % ways) for d in range(ways)])
+        full = lax.dynamic_update_slice_in_dim(full, going_up, (here - far) % ways * lap, axis=dim)
+        if 2 * far < ways:
+            going_down = lax.ppermute(going_down, axis, [(d, (d - 1) % ways) for d in range(ways)])
+            full = lax.dynamic_update_slice_in_dim(
+                full, going_down, (here + far) % ways * lap, axis=dim
+            )
+    return full
 
 
 def per_device(
@@ -51,9 +69,7 @@
         ).astype(jnp.bfloat16)
         per_head = per_head.reshape(per_head.shape[0], per_head.shape[1] * per_head.shape[2])
         partial_sums = jnp.dot(
-            lax.all_gather(per_head, "group", axis=0, tiled=True),
-            out_proj,
-            preferred_element_type=jnp.float32,
+            gather_around(per_head, "group", 0), out_proj, preferred_element_type=jnp.float32
         )
         arrived_sums = lax.all_to_all(
             partial_sums.astype(jnp.bfloat16).reshape(members, -1, columns),

time: 238 us -> 228 us (0.958)
  starting transfers between devices: 19.2 us -> 44.4 us
  blocking collectives: 68.6 us -> 47 us
  between operations: 13.7 us -> 0.66 us
  local copies, waits for them, and re-layouts: 33.5 us -> 36.9 us
  matrix products: 32.7 us -> 30 us
    all_to_all x2 -> x0, blocking collectives: 31.1 us -> none  [per_device(): lax.all_to_all(latent_out, 'member', split_axis=1, concat_axis=0, tiled=T...]
    all_gather x2 -> x0, waiting for transfers between devices: 20.2 us -> none  [per_device(): lax.all_gather(per_head, 'group', axis=0, tiled=True)]
    ppermute x0 -> x14, starting transfers between devices: none -> 18.9 us  [the longest x8 14.4 us: gather_around(): lax.ppermute(going_up, axis, [(d, (d + 1) % ways) for d in range(ways)])]
    all_to_all x0 -> x2, starting transfers between devices: none -> 12 us  [per_device(): lax.all_to_all(latent_out, 'member', split_axis=1, concat_axis=0, tiled=T...]
    all_to_all x0 -> x2, waiting for transfers between devices: none -> 9.89 us  [per_device(): lax.all_to_all(latent_out, 'member', split_axis=1, concat_axis=0, tiled=T...]
    all_to_all x1, blocking collectives: 37.5 us -> 47 us  [per_device(): lax.all_to_all(outgoing.reshape(experts, capacity, columns), ('group', 'm...]
    all_to_all x2, starting transfers between devices: 13.4 us -> 7.64 us  [per_device(): lax.all_to_all(partial_sums.astype(jnp.bfloat16).reshape(members, -1, col...]
    ppermute x0 -> x14, waiting for transfers between devices: none -> 5.57 us  [the longest x8 4.69 us: gather_around(): lax.ppermute(going_up, axis, [(d, (d + 1) % ways) for d in range(ways)])]
  transfers between devices with their start and end apart: 5 -> 19, of which waited for: 4 -> 11; matrix products, arithmetic and copies ran while one was open for 9% -> 9% of each run, Pallas kernels for 0% -> 0%
where the time goes in v1:
time: 228 us; the launch traced here: 227 us
  waiting for transfers between devices  54.7 us (24%)
  blocking collectives  47 us (21%)
  starting transfers between devices  44.4 us (19%)
  local copies, waits for them, and re-layouts  36.9 us (16%)
  matrix products  30 us (13%)
  other arithmetic  13.5 us (6%)
    all_to_all x1, blocking collectives, per_device(): lax.all_to_all(outgoing.reshape(experts, capacity, columns), ('group', 'm...  47 us
    all_to_all x1, waiting for transfers between devices, per_device(): lax.all_to_all(arranged, ('group', 'member'), split_axis=0, concat_axis=0...  28.5 us
    ppermute x8, starting transfers between devices, gather_around(): lax.ppermute(going_up, axis, [(d, (d + 1) % ways) for d in range(ways)])  14.4 us
    all_to_all x2, starting transfers between devices, per_device(): lax.all_to_all(latent_out, 'member', split_axis=1, concat_axis=0, tiled=T...  12 us
    all_to_all x2, waiting for transfers between devices, per_device(): lax.all_to_all(partial_sums.astype(jnp.bfloat16).reshape(members, -1, col...  10.8 us
    dot_general x1, matrix products, per_device(): jnp.dot(inner, w_down[0], preferred_element_type=jnp.float32)  10.8 us
    all_to_all x2, waiting for transfers between devices, per_device(): lax.all_to_all(latent_out, 'member', split_axis=1, concat_axis=0, tiled=T...  9.89 us
    all_to_all x2, starting transfers between devices, per_device(): lax.all_to_all(partial_sums.astype(jnp.bfloat16).reshape(members, -1, col...  7.64 us
  transfers between devices with their start and end apart: 19, of which 11 were waited for; matrix products, arithmetic and copies ran while one was open for 9% of the time, Pallas kernels for 0%

profile of v1, /device:TPU:1, one launch (start us, length us, event | category | flops | bytes accessed | tf_op | source)
XLA Modules:
  0.0 227.1 jit_solution(10429592168810431629)
XLA Ops:
  3.9 4.4 %copy.88 = bf16[16,128,576]{2,1,0:T(8,128)(2,1)} copy(bf16[16,128,576]{1,2,0:T(8,128)(2,1)} %gather_fusion) | data formatting | bytes 4718592 | tf_op jit(solution)/shard_map/jit(_take)/gather | solution.py:53
  15.7 8.4 %all-to-all-start = ((bf16[8,64,512]{2,0,1:T(8,128)(2,1)}), bf16[8,64,512]{2,0,1:T(8,128)(2,1)S(1)}, u32[]{:S(2)}, u32[]{:S(2)}) async-start(bf16[8,64,512]{2,0,1:T(8,128)(2,1)} %copy.90), calls=%async_computation | async-start | bytes 1048576 | tf_op jit(solution)/shard_map/all_to_all | solution.py:66
  26.6 2.3 %convolution_convert_fusion.3 = bf16[8,64,512]{2,1,0:T(8,128)(2,1)S(1)} fusion(bf16[16,1,576]{2,1,0:T(2,128)(2,1)S(1)} %copy.89, bf16[16,128,576]{2,1,0:T(8,128)(2,1)} %copy-done.2, f32[8,64]{1,0:T(8,128)S(1)} %fusion.61, f32[8,64,129]{2,1,0:T(8,128)S(1)} %fusion.28), kind=kOutput, calls=%fused_computation.27 | convolution fusion | flops 70207616 | bytes 3168256 | tf_op jit(solution)/shard_map/rhc,rcl->rhl/dot_general | solution.py:63
  30.0 4.5 %all-to-all-done = bf16[8,64,512]{2,0,1:T(8,128)(2,1)S(1)} async-done(((bf16[8,64,512]{2,0,1:T(8,128)(2,1)}), bf16[8,64,512]{2,0,1:T(8,128)(2,1)S(1)}, u32[]{:S(2)}, u32[]{:S(2)}) %all-to-all-start) | async-done | bytes 524320 | tf_op jit(solution)/shard_map/all_to_all | solution.py:66
  34.5 3.6 %all-to-all-start.2 = ((bf16[8,64,512]{2,0,1:T(8,128)(2,1)}), bf16[8,64,512]{2,0,1:T(8,128)(2,1)S(1)}, u32[]{:S(2)}, u32[]{:S(2)}) async-start(bf16[8,64,512]{2,0,1:T(8,128)(2,1)} %copy.94), calls=%async_computation.2 | async-start | bytes 1048576 | tf_op jit(solution)/shard_map/all_to_all | solution.py:66
  38.6 3.3 %collective-permute-start = (bf16[128,512]{0,1:T(8,128)(2,1)S(1)}, bf16[128,512]{0,1:T(8,128)(2,1)S(1)}, u32[]{:S(2)}, u32[]{:S(2)}) collective-permute-start(bf16[128,512]{0,1:T(8,128)(2,1)S(1)} %bitcast.94), channel_id=1, source_target_pairs={{0,16},{16,32},{32,48},{48,64},{64,80},{80,96},{96,112},{112,0},{1... | collective-permute-start | bytes 393224 | tf_op jit(solution)/shard_map/ppermute | solution.py:20
  41.8 5.4 %all-to-all-done.2 = bf16[8,64,512]{2,0,1:T(8,128)(2,1)S(1)} async-done(((bf16[8,64,512]{2,0,1:T(8,128)(2,1)}), bf16[8,64,512]{2,0,1:T(8,128)(2,1)S(1)}, u32[]{:S(2)}, u32[]{:S(2)}) %all-to-all-start.2) | async-done | bytes 524320 | tf_op jit(solution)/shard_map/all_to_all | solution.py:66
  47.6 4.5 %collective-permute-start.7 = (bf16[128,512]{0,1:T(8,128)(2,1)S(1)}, bf16[128,512]{0,1:T(8,128)(2,1)S(1)}, u32[]{:S(2)}, u32[]{:S(2)}) collective-permute-start(bf16[128,512]{0,1:T(8,128)(2,1)S(1)} %bitcast.91), channel_id=1, source_target_pairs={{0,16},{16,32},{32,48},{48,64},{64,80},{80,96},{96,112},{112,0},{1... | collective-permute-start | bytes 393224 | tf_op jit(solution)/shard_map/ppermute | solution.py:20
  67.3 2.4 %collective-permute-done.13 = bf16[128,512]{0,1:T(8,128)(2,1)S(1)} collective-permute-done((bf16[128,512]{0,1:T(8,128)(2,1)S(1)}, bf16[128,512]{0,1:T(8,128)(2,1)S(1)}, u32[]{:S(2)}, u32[]{:S(2)}) %collective-permute-start.13) | collective-permute-done | bytes 131104 | tf_op jit(solution)/shard_map/ppermute | solution.py:20
  71.8 3.8 %all-to-all-start.3 = ((bf16[16,64,448]{2,1,0:T(8,128)(2,1)}), bf16[16,64,448]{2,1,0:T(8,128)(2,1)S(1)}, u32[]{:S(2)}, u32[]{:S(2)}) async-start(bf16[16,64,448]{2,1,0:T(8,128)(2,1)} %bitcast.17), calls=%async_computation.3 | async-start | bytes 2097152 | tf_op jit(solution)/shard_map/all_to_all | solution.py:74
  77.8 2.3 %copy.93 = bf16[1024,448]{1,0:T(8,128)(2,1)} copy(bf16[1024,448]{0,1:T(8,128)(2,1)} %convolution_convert_fusion.2) | data formatting | bytes 1835008 | tf_op jit(solution)/shard_map/convert_element_type | solution.py:75
  80.1 7.6 %all-to-all-done.3 = bf16[16,64,448]{2,1,0:T(8,128)(2,1)S(1)} async-done(((bf16[16,64,448]{2,1,0:T(8,128)(2,1)}), bf16[16,64,448]{2,1,0:T(8,128)(2,1)S(1)}, u32[]{:S(2)}, u32[]{:S(2)}) %all-to-all-start.3) | async-done | bytes 917536 | tf_op jit(solution)/shard_map/all_to_all | solution.py:74
  87.7 3.9 %all-to-all-start.1 = ((bf16[16,64,448]{2,1,0:T(8,128)(2,1)}), bf16[16,64,448]{2,1,0:T(8,128)(2,1)S(1)}, u32[]{:S(2)}, u32[]{:S(2)}) async-start(bf16[16,64,448]{2,1,0:T(8,128)(2,1)} %bitcast.8), calls=%async_computation.1 | async-start | bytes 2097152 | tf_op jit(solution)/shard_map/all_to_all | solution.py:74
  92.4 7.4 %fusion.2 = pred[2048,128]{1,0:T(8,128)(4,1)S(1)} fusion(s32[128,8]{0,1:T(8,128)S(1)} %get-tuple-element.6), kind=kLoop, calls=%fused_computation.5 | loop fusion | flops 3932160 | bytes 266240 | tf_op jit(solution)/shard_map/reduce_or | solution.py:95
  100.0 3.2 %all-to-all-done.1 = bf16[16,64,448]{2,1,0:T(8,128)(2,1)S(1)} async-done(((bf16[16,64,448]{2,1,0:T(8,128)(2,1)}), bf16[16,64,448]{2,1,0:T(8,128)(2,1)S(1)}, u32[]{:S(2)}, u32[]{:S(2)}) %all-to-all-start.1) | async-done | bytes 917536 | tf_op jit(solution)/shard_map/all_to_all | solution.py:74
  105.5 2.8 %copy.105 = bf16[2048,448]{1,0:T(8,128)(2,1)S(1)} copy(bf16[2048,448]{0,1:T(8,128)(2,1)} %convolution_convert_fusion) | data formatting | bytes 3670016 | tf_op jit(solution)/shard_map/convert_element_type | solution.py:96
  108.3 47.0 %all_to_all.56 = bf16[128,16,448]{2,1,0:T(8,128)(2,1)S(1)} all-to-all(bf16[128,16,448]{2,1,0:T(8,128)(2,1)S(1)} %bitcast.86), channel_id=1, replica_groups=mesh['group'=8,'member'=16] {'group','member'}, dimensions={0} | all-to-all | bytes 3670016 | tf_op jit(solution)/shard_map/all_to_all | solution.py:97
  156.6 3.3 %reshape.88 = bf16[256,3584]{1,0:T(8,128)(2,1)} reshape(bf16[16,16,8,448]{3,2,1,0:T(8,128)(2,1)S(1)} %bitcast.88) | data formatting | bytes 3670016 | tf_op jit(solution)/shard_map/reshape | solution.py:107
  159.9 6.8 %fusion.7 = f32[256,1024]{1,0:T(8,128)} fusion(bf16[256,3584]{1,0:T(8,128)(2,1)} %reshape.88, bf16[1,3584,1024]{2,1,0:T(8,128)(2,1)} %param.21), kind=kOutput, calls=%fused_computation.10 | convolution fusion | flops 1879048192 | bytes 10223616 | tf_op jit(solution)/shard_map/dot_general | solution.py:109
  166.8 10.8 %fusion.9 = bf16[256,3584]{1,0:T(8,128)(2,1)} fusion(bf16[1,1024,3584]{2,1,0:T(8,128)(2,1)} %param.23, bf16[256,3584]{1,0:T(8,128)(2,1)S(1)} %copy-done.4, bf16[1,3584,1024]{2,1,0:T(8,128)(2,1)} %param.22, f32[256,1024]{1,0:T(8,128)} %fusion.7), kind=kOutput, calls=%fused_computation.12 | convolution fusion | flops 3760586752 | bytes 19398656 | tf_op jit(solution)/shard_map/dot_general | solution.py:112
  177.6 3.9 %reshape.89 = bf16[16,16,8,448]{3,2,1,0:T(8,128)(2,1)S(1)} reshape(bf16[256,3584]{1,0:T(8,128)(2,1)} %fusion.9) | data formatting | bytes 3670016 | tf_op jit(solution)/shard_map/reshape | solution.py:114
  183.5 5.9 %all-to-all-start.5 = ((bf16[128,16,448]{2,1,0:T(8,128)(2,1)}), bf16[128,16,448]{2,1,0:T(8,128)(2,1)}, u32[]{:S(2)}, u32[]{:S(2)}) async-start(bf16[128,16,448]{2,1,0:T(8,128)(2,1)} %bitcast.30), calls=%async_computation.5 | async-start | bytes 4194304 | tf_op jit(solution)/shard_map/all_to_all | solution.py:118
  190.3 28.5 %all-to-all-done.5 = bf16[128,16,448]{2,1,0:T(8,128)(2,1)} async-done(((bf16[128,16,448]{2,1,0:T(8,128)(2,1)}), bf16[128,16,448]{2,1,0:T(8,128)(2,1)}, u32[]{:S(2)}, u32[]{:S(2)}) %all-to-all-start.5) | async-done | bytes 1835040 | tf_op jit(solution)/shard_map/all_to_all | solution.py:118
  218.8 6.0 %gather_fusion.1 = bf16[1024,448]{1,0:T(8,128)(2,1)S(1)} fusion(bf16[2048,448]{1,0:T(8,128)(2,1)} %bitcast.31, s32[1024]{0:T(1024)S(1)} %broadcast_clamp_fusion), kind=kCustom, calls=%fused_computation.1 | custom fusion | bytes 1839104 | tf_op jit(solution)/shard_map/gather | solution.py:122
  (113 shorter events, 44.7 us)
Async XLA Ops:
  15.7 18.8 %all-to-all-start = ((bf16[8,64,512]{2,0,1:T(8,128)(2,1)}), bf16[8,64,512]{2,0,1:T(8,128)(2,1)S(1)}, u32[]{:S(2)}, u32[]{:S(2)}) async-start(bf16[8,64,512]{2,0,1:T(8,128)(2,1)} %copy.90), calls=%async_computation | async-start | bytes 1048576 | tf_op jit(solution)/shard_map/all_to_all | solution.py:66
  26.5 11.7 %copy-start.3 = (bf16[4,512,128]{2,1,0:T(8,128)(2,1)S(1)}, bf16[4,512,128]{2,1,0:T(8,128)(2,1)}, u32[]{:S(2)}) copy-start(bf16[4,512,128]{2,1,0:T(8,128)(2,1)} %param.16) | copy-start | bytes 1572868
  34.5 12.7 %all-to-all-start.2 = ((bf16[8,64,512]{2,0,1:T(8,128)(2,1)}), bf16[8,64,512]{2,0,1:T(8,128)(2,1)S(1)}, u32[]{:S(2)}, u32[]{:S(2)}) async-start(bf16[8,64,512]{2,0,1:T(8,128)(2,1)} %copy.94), calls=%async_computation.2 | async-start | bytes 1048576 | tf_op jit(solution)/shard_map/all_to_all | solution.py:66
  38.6 13.8 %collective-permute-start = (bf16[128,512]{0,1:T(8,128)(2,1)S(1)}, bf16[128,512]{0,1:T(8,128)(2,1)S(1)}, u32[]{:S(2)}, u32[]{:S(2)}) collective-permute-start(bf16[128,512]{0,1:T(8,128)(2,1)S(1)} %bitcast.94), channel_id=1, source_target_pairs={{0,16},{16,32},{32,48},{48,64},{64,80},{80,96},{96,112},{112,0},{1... | collective-permute-start | bytes 393224 | tf_op jit(solution)/shard_map/ppermute | solution.py:20
  41.8 12.3 %collective-permute-start.1 = (bf16[128,512]{0,1:T(8,128)(2,1)S(1)}, bf16[128,512]{0,1:T(8,128)(2,1)S(1)}, u32[]{:S(2)}, u32[]{:S(2)}) collective-permute-start(bf16[128,512]{0,1:T(8,128)(2,1)S(1)} %bitcast.95), channel_id=1, source_target_pairs={{0,112},{16,0},{32,16},{48,32},{64,48},{80,64},{96,80},{112,96},{1... | collective-permute-start | bytes 393224 | tf_op jit(solution)/shard_map/ppermute | solution.py:23
  47.6 6.7 %collective-permute-start.7 = (bf16[128,512]{0,1:T(8,128)(2,1)S(1)}, bf16[128,512]{0,1:T(8,128)(2,1)S(1)}, u32[]{:S(2)}, u32[]{:S(2)}) collective-permute-start(bf16[128,512]{0,1:T(8,128)(2,1)S(1)} %bitcast.91), channel_id=1, source_target_pairs={{0,16},{16,32},{32,48},{48,64},{64,80},{80,96},{96,112},{112,0},{1... | collective-permute-start | bytes 393224 | tf_op jit(solution)/shard_map/ppermute | solution.py:20
  52.0 4.5 %collective-permute-start.8 = (bf16[128,512]{0,1:T(8,128)(2,1)S(1)}, bf16[128,512]{0,1:T(8,128)(2,1)S(1)}, u32[]{:S(2)}, u32[]{:S(2)}) collective-permute-start(bf16[128,512]{0,1:T(8,128)(2,1)S(1)} %bitcast.92), channel_id=1, source_target_pairs={{0,112},{16,0},{32,16},{48,32},{64,48},{80,64},{96,80},{112,96},{1... | collective-permute-start | bytes 393224 | tf_op jit(solution)/shard_map/ppermute | solution.py:23
  52.2 17.6 %copy-start.10 = (bf16[512,448]{0,1:T(8,128)(2,1)S(1)}, bf16[512,448]{0,1:T(8,128)(2,1)}, u32[]{:S(2)}) copy-start(bf16[512,448]{0,1:T(8,128)(2,1)} %param.17) | copy-start | bytes 1376260
  52.4 5.0 %collective-permute-start.2 = (bf16[128,512]{0,1:T(8,128)(2,1)S(1)}, bf16[128,512]{0,1:T(8,128)(2,1)S(1)}, u32[]{:S(2)}, u32[]{:S(2)}) collective-permute-start(bf16[128,512]{0,1:T(8,128)(2,1)S(1)} %collective-permute-done), channel_id=1, source_target_pairs={{0,16},{16,32},{32,48},{48,64},{64,80},{80,96},{96,112},{112,0},{1... | collective-permute-start | bytes 393224 | tf_op jit(solution)/shard_map/ppermute | solution.py:20
  54.1 4.7 %collective-permute-start.3 = (bf16[128,512]{0,1:T(8,128)(2,1)S(1)}, bf16[128,512]{0,1:T(8,128)(2,1)S(1)}, u32[]{:S(2)}, u32[]{:S(2)}) collective-permute-start(bf16[128,512]{0,1:T(8,128)(2,1)S(1)} %collective-permute-done.1), channel_id=1, source_target_pairs={{0,112},{16,0},{32,16},{48,32},{64,48},{80,64},{96,80},{112,96},{1... | collective-permute-start | bytes 393224 | tf_op jit(solution)/shard_map/ppermute | solution.py:23
  54.2 6.2 %collective-permute-start.9 = (bf16[128,512]{0,1:T(8,128)(2,1)S(1)}, bf16[128,512]{0,1:T(8,128)(2,1)S(1)}, u32[]{:S(2)}, u32[]{:S(2)}) collective-permute-start(bf16[128,512]{0,1:T(8,128)(2,1)S(1)} %collective-permute-done.7), channel_id=1, source_target_pairs={{0,16},{16,32},{32,48},{48,64},{64,80},{80,96},{96,112},{112,0},{1... | collective-permute-start | bytes 393224 | tf_op jit(solution)/shard_map/ppermute | solution.py:20
  56.5 4.7 %collective-permute-start.10 = (bf16[128,512]{0,1:T(8,128)(2,1)S(1)}, bf16[128,512]{0,1:T(8,128)(2,1)S(1)}, u32[]{:S(2)}, u32[]{:S(2)}) collective-permute-start(bf16[128,512]{0,1:T(8,128)(2,1)S(1)} %collective-permute-done.8), channel_id=1, source_target_pairs={{0,112},{16,0},{32,16},{48,32},{64,48},{80,64},{96,80},{112,96},{1... | collective-permute-start | bytes 393224 | tf_op jit(solution)/shard_map/ppermute | solution.py:23
  57.4 6.1 %collective-permute-start.4 = (bf16[128,512]{0,1:T(8,128)(2,1)S(1)}, bf16[128,512]{0,1:T(8,128)(2,1)S(1)}, u32[]{:S(2)}, u32[]{:S(2)}) collective-permute-start(bf16[128,512]{0,1:T(8,128)(2,1)S(1)} %collective-permute-done.2), channel_id=1, source_target_pairs={{0,16},{16,32},{32,48},{48,64},{64,80},{80,96},{96,112},{112,0},{1... | collective-permute-start | bytes 393224 | tf_op jit(solution)/shard_map/ppermute | solution.py:20
  58.8 6.5 %collective-permute-start.5 = (bf16[128,512]{0,1:T(8,128)(2,1)S(1)}, bf16[128,512]{0,1:T(8,128)(2,1)S(1)}, u32[]{:S(2)}, u32[]{:S(2)}) collective-permute-start(bf16[128,512]{0,1:T(8,128)(2,1)S(1)} %collective-permute-done.3), channel_id=1, source_target_pairs={{0,112},{16,0},{32,16},{48,32},{64,48},{80,64},{96,80},{112,96},{1... | collective-permute-start | bytes 393224 | tf_op jit(solution)/shard_map/ppermute | solution.py:23
  60.4 3.8 %collective-permute-start.11 = (bf16[128,512]{0,1:T(8,128)(2,1)S(1)}, bf16[128,512]{0,1:T(8,128)(2,1)S(1)}, u32[]{:S(2)}, u32[]{:S(2)}) collective-permute-start(bf16[128,512]{0,1:T(8,128)(2,1)S(1)} %collective-permute-done.9), channel_id=1, source_target_pairs={{0,16},{16,32},{32,48},{48,64},{64,80},{80,96},{96,112},{112,0},{1... | collective-permute-start | bytes 393224 | tf_op jit(solution)/shard_map/ppermute | solution.py:20
  61.2 4.4 %collective-permute-start.12 = (bf16[128,512]{0,1:T(8,128)(2,1)S(1)}, bf16[128,512]{0,1:T(8,128)(2,1)S(1)}, u32[]{:S(2)}, u32[]{:S(2)}) collective-permute-start(bf16[128,512]{0,1:T(8,128)(2,1)S(1)} %collective-permute-done.10), channel_id=1, source_target_pairs={{0,112},{16,0},{32,16},{48,32},{64,48},{80,64},{96,80},{112,96},{1... | collective-permute-start | bytes 393224 | tf_op jit(solution)/shard_map/ppermute | solution.py:23
  63.5 3.8 %collective-permute-start.6 = (bf16[128,512]{0,1:T(8,128)(2,1)S(1)}, bf16[128,512]{0,1:T(8,128)(2,1)S(1)}, u32[]{:S(2)}, u32[]{:S(2)}) collective-permute-start(bf16[128,512]{0,1:T(8,128)(2,1)S(1)} %collective-permute-done.4), channel_id=1, source_target_pairs={{0,16},{16,32},{32,48},{48,64},{64,80},{80,96},{96,112},{112,0},{1... | collective-permute-start | bytes 393224 | tf_op jit(solution)/shard_map/ppermute | solution.py:20
  64.1 5.6 %collective-permute-start.13 = (bf16[128,512]{0,1:T(8,128)(2,1)S(1)}, bf16[128,512]{0,1:T(8,128)(2,1)S(1)}, u32[]{:S(2)}, u32[]{:S(2)}) collective-permute-start(bf16[128,512]{0,1:T(8,128)(2,1)S(1)} %collective-permute-done.11), channel_id=1, source_target_pairs={{0,16},{16,32},{32,48},{48,64},{64,80},{80,96},{96,112},{112,0},{1... | collective-permute-start | bytes 393224 | tf_op jit(solution)/shard_map/ppermute | solution.py:20
  71.8 15.8 %all-to-all-start.3 = ((bf16[16,64,448]{2,1,0:T(8,128)(2,1)}), bf16[16,64,448]{2,1,0:T(8,128)(2,1)S(1)}, u32[]{:S(2)}, u32[]{:S(2)}) async-start(bf16[16,64,448]{2,1,0:T(8,128)(2,1)} %bitcast.17), calls=%async_computation.3 | async-start | bytes 2097152 | tf_op jit(solution)/shard_map/all_to_all | solution.py:74
  77.8 13.9 %copy-start.5 = (bf16[128,448]{0,1:T(8,128)(2,1)S(1)}, bf16[128,448]{0,1:T(8,128)(2,1)}, u32[]{:S(2)}) copy-start(bf16[128,448]{0,1:T(8,128)(2,1)} %param.18) | copy-start | bytes 344068
  87.7 15.6 %all-to-all-start.1 = ((bf16[16,64,448]{2,1,0:T(8,128)(2,1)}), bf16[16,64,448]{2,1,0:T(8,128)(2,1)S(1)}, u32[]{:S(2)}, u32[]{:S(2)}) async-start(bf16[16,64,448]{2,1,0:T(8,128)(2,1)} %bitcast.8), calls=%async_computation.1 | async-start | bytes 2097152 | tf_op jit(solution)/shard_map/all_to_all | solution.py:74
  159.9 6.8 %copy-start.4 = (bf16[256,3584]{1,0:T(8,128)(2,1)S(1)}, bf16[256,3584]{1,0:T(8,128)(2,1)}, u32[]{:S(2)}) copy-start(bf16[256,3584]{1,0:T(8,128)(2,1)} %reshape.88) | copy-start | bytes 5505028
  183.5 35.3 %all-to-all-start.5 = ((bf16[128,16,448]{2,1,0:T(8,128)(2,1)}), bf16[128,16,448]{2,1,0:T(8,128)(2,1)}, u32[]{:S(2)}, u32[]{:S(2)}) async-start(bf16[128,16,448]{2,1,0:T(8,128)(2,1)} %bitcast.30), calls=%async_computation.5 | async-start | bytes 4194304 | tf_op jit(solution)/shard_map/all_to_all | solution.py:118
  218.8 8.4 %copy-start.1 = (bf16[16,128,576]{1,2,0:T(8,128)(2,1)S(1)}, bf16[16,128,576]{1,2,0:T(8,128)(2,1)}, u32[]{:S(2)}) copy-start(bf16[16,128,576]{1,2,0:T(8,128)(2,1)} %param.13) | copy-start | bytes 7077892
  (7 other events, 25.3 us)
